TPU v7x, 128 devices: a whole 4x4x4 slice. The times are simulated.
128 devices in a mesh: prow: 16 (over y, x_hi, core), pcol: 8 (over x_lo, z).
Axes of the slice: x: 4 (x_hi: 2, x_lo: 2; x = x_hi * 2 + x_lo), y: 4, z: 4, core: 2. Of those that a mesh axis runs over, the one named last changes fastest.
Arguments:
- inverse_block: float32 [3, 16, 256, 6, 8, 256], P(None, 'prow', None, None, 'pcol'), as said below
- panel_first: float32 [3, 16, 256, 512], P(None, 'prow', 'pcol'), may hold values from -0.0546875 to 0.0546875
- panel_second: float32 [3, 16, 256, 512], P(None, 'prow', 'pcol'), may hold values from -0.0546875 to 0.0546875
- diag_first: float32 [512, 512], replicated, may hold values from -6 to 6
- diag_second: float32 [512, 512], replicated, may hold values from -6 to 6
- pattern_first: int32 [48], replicated, may hold values from 0 to 1, as said below
- pattern_second: int32 [48], replicated, may hold values from 0 to 1, as said below
Outputs:
- column_first: float32 [3, 16, 256, 512], P(None, 'prow', 'pcol')
- column_second: float32 [3, 16, 256, 512], P(None, 'prow', 'pcol')
- diagonal_first: float32 [512, 512], replicated
- diagonal_second: float32 [512, 512], replicated
Inputs may be any that keep to these rules, and one draw needn't show every extreme that they name: inverse_block is symmetric as a matrix of 12288 rows: its entry (i, j) equals its entry (j, i) exactly. `pattern_first`: at least one entry is 1. `pattern_second`: at least one entry is 1.
All inputs are finite; a program needn't handle non-finite values.
Results may differ from a plain program's by a relative error of at most 0.000071.
Values sent between devices are 32-bit elements; how exact they have to be, the bound alone decides.
No kernel may reach another device: no remote copies, remote signals or barrier semaphores. Data moves between devices by JAX's collectives and lax.ppermute only.
A program may use at most 64 MiB of HBM per device.

v0:
```python
import jax
import jax.numpy as jnp
from jax import lax
from jax.sharding import PartitionSpec as P


TILE = 128
PIECE = 512


def pack_upper(d):
    n = d.shape[-1] // TILE
    blocks = [
        d[..., i * TILE:(i + 1) * TILE, j * TILE:(j + 1) * TILE]
        for i in range(n)
        for j in range(i, n)
    ]
    return jnp.stack(blocks, axis=-3)


def unpack_upper(packed, n):
    rows = [[None] * n for _ in range(n)]
    k = 0
    for i in range(n):
        for j in range(i, n):
            blk = packed[..., k, :, :]
            rows[i][j] = blk
            if i != j:
                rows[j][i] = jnp.swapaxes(blk, -1, -2)
            k += 1
    return jnp.concatenate([jnp.concatenate(r, axis=-1) for r in rows], axis=-2)


def body(
    inverse_block, panel_first, panel_second, diag_first, diag_second, pattern_first, pattern_second
):
    prow = ("prow_hi", "core")
    row_count = lax.axis_size(prow)
    pair = lax.axis_size("core")
    core = lax.axis_index("core")
    col_count = lax.axis_size("pcol")
    row_index = lax.axis_index(prow)
    col_index = lax.axis_index("pcol")
    row_blocks = inverse_block.shape[0]
    block_rows = inverse_block.shape[2]
    col_blocks = inverse_block.shape[3]
    slice_rows = panel_first.shape[2]
    width = panel_first.shape[3]
    highest = lax.Precision.HIGHEST
    both = ("prow_hi", "core", "pcol")
    swap = [(b, (b + 1) % pair) for b in range(pair)]

    def pair_sum(value, axis):
        split = value.reshape(value.shape[:axis] + (value.shape[axis] // pair, pair) + value.shape[axis + 1:])
        mine = lax.dynamic_index_in_dim(split, core, axis + 1, False)
        other = lax.dynamic_index_in_dim(split, (core + 1) % pair, axis + 1, False)
        return mine + lax.ppermute(other, "core", swap)

    def kept_of(pattern, prow):
        return lax.dynamic_index_in_dim(
            pattern.reshape(row_blocks, row_count), prow, 1, False
        ).astype(jnp.float32)

    own_first = kept_of(pattern_first, row_index)
    own_second = kept_of(pattern_second, row_index)
    x = jnp.concatenate(
        [
            panel_first[:, 0] * own_first[:, None, None],
            panel_second[:, 0] * own_second[:, None, None],
        ],
        axis=-1,
    )

    to_reducer = []
    to_owner = []
    for q in range(row_count):
        for c in range(col_count):
            reducer = (col_count * (q // col_count) + c) * col_count + q % col_count
            to_reducer.append((q * col_count + c, reducer))
            to_owner.append((reducer, q * col_count + c))
    x_at_reducer = lax.ppermute(x, both, to_reducer)

    matrix = inverse_block.reshape(row_blocks, block_rows, col_blocks, block_rows)

    def reduce_inner(piece, by_permutes):
        gathered = gather_piece(piece, by_permutes)
        return reduce_gathered(piece, gathered)

    def gather_piece(piece, by_permutes):
        if by_permutes:
            bits = col_count.bit_length() - 1
            order = [1, 0, 2] if bits == 3 else list(range(bits))
            held = piece
            axes = []
            for b in order:
                mine = (col_index >> b) & 1
                got = lax.ppermute(held, "pcol", [(i, i ^ (1 << b)) for i in range(col_count)])
                pos = sum(1 for a in axes if a > b)
                held = jnp.where(
                    mine == 0,
                    jnp.stack([held, got], axis=pos),
                    jnp.stack([got, held], axis=pos),
                )
                axes.insert(pos, b)
            gathered = jnp.moveaxis(
                held.reshape((col_count,) + piece.shape), 0, 1
            ).reshape(row_blocks, block_rows, piece.shape[-1])
        else:
            spread = jnp.broadcast_to(
                piece[:, None], (row_blocks, col_count) + piece.shape[1:]
            ).reshape(row_blocks, block_rows, piece.shape[-1])
            gathered = lax.all_to_all(spread, "pcol", 1, 1, tiled=True)
        return gathered

    def reduce_gathered(piece, gathered):
        partial = product_of(gathered)
        chunks = partial.reshape(row_blocks, row_count, slice_rows, piece.shape[-1])
        pre = pair_sum(chunks, 1)
        received = lax.all_to_all(pre, "prow_hi", 1, 1, tiled=True)
        return jnp.sum(received, axis=1)

    def product_of(gathered):
        return jnp.einsum(
            "lsmt,lsw->mtw",
            matrix,
            gathered,
            precision=highest,
            preferred_element_type=jnp.float32,
        )

    total = jnp.concatenate(
        [
            reduce_inner(x[..., k * PIECE:(k + 1) * PIECE], k > 0)
            for k in range(2 * width // PIECE)
        ],
        axis=-1,
    )

    owner_row = col_index + col_count * (row_index // col_count)
    kept_first = kept_of(pattern_first, owner_row)
    kept_second = kept_of(pattern_second, owner_row)
    column = jnp.concatenate(
        [
            -(total[..., :width] * kept_first[:, None, None]),
            -(total[..., width:] * kept_second[:, None, None]),
        ],
        axis=-1,
    )
    parts = jnp.stack(
        [
            jnp.einsum(
                "lsw,lsv->wv",
                x_at_reducer[..., :width],
                column[..., :width],
                precision=highest,
                preferred_element_type=jnp.float32,
            ),
            jnp.einsum(
                "lsw,lsv->wv",
                x_at_reducer[..., width:],
                column[..., width:],
                precision=highest,
                preferred_element_type=jnp.float32,
            ),
        ]
    )
    column_home = lax.ppermute(column, both, to_owner)
    packed = pack_upper(parts)
    others = ("prow_hi", "pcol")
    devices = lax.axis_size(others)
    half = pair_sum(packed.reshape(pair * devices, packed.size // (pair * devices)), 0)
    flat = half.reshape(devices, half.size // devices)
    reduced = jnp.sum(lax.all_to_all(flat, others, 0, 0, tiled=True), axis=0)
    spread_sum = jnp.broadcast_to(reduced[None], flat.shape)
    mine = lax.all_to_all(spread_sum, others, 0, 0, tiled=True).reshape(half.shape)
    other = lax.ppermute(mine, "core", swap)
    summed = jnp.where(
        core == 0,
        jnp.stack([mine, other], axis=1),
        jnp.stack([other, mine], axis=1),
    ).reshape(packed.shape)
    sums = unpack_upper(summed, width // TILE)
    return (
        column_home[:, None, :, :width],
        column_home[:, None, :, width:],
        diag_first - sums[0],
        diag_second - sums[1],
    )


def solution(mesh):
    rows, cols = mesh.devices.shape
    split = jax.sharding.Mesh(mesh.devices.reshape(rows // 2, 2, cols), ("prow_hi", "core", "pcol"))
    prow = ("prow_hi", "core")
    placed = (
        P(None, prow, None, None, "pcol", None),
        P(None, prow, "pcol", None),
        P(None, prow, "pcol", None),
        P(),
        P(),
        P(),
        P(),
    )

    return jax.shard_map(
        body,
        mesh=split,
        in_specs=placed,
        out_specs=(P(None, prow, "pcol", None), P(None, prow, "pcol", None), P(), P()),
        check_vma=False,
    )
```

profile of v0, /device:TPU:6, one launch (start us, length us, event | category | flops | bytes accessed | tf_op | source)
XLA Modules:
  0.0 232.2 jit_solution(6822407111641995977)
XLA Ops:
  3.4 4.0 %collective-permute-start.1 = (f32[3,32,512]{2,1,0:T(8,128)S(1)}, f32[3,32,512]{2,1,0:T(8,128)S(1)}, u32[]{:S(2)}, u32[]{:S(2)}) collective-permute-start(f32[3,32,512]{2,1,0:T(8,128)S(1)} %bitcast_multiply_fusion.1), channel_id=1, source_target_pairs={{0,2},{1,3},{2,0},{3,1},{4,6},{5,7},{6,4},{7,5},{8,10},{9,11},{10,... | collective-permute-start | bytes 589832 | tf_op jit(solution)/shard_map/ppermute | solution.py:97
  8.4 3.9 %collective-permute-done.1 = f32[3,32,512]{2,1,0:T(8,128)S(1)} collective-permute-done((f32[3,32,512]{2,1,0:T(8,128)S(1)}, f32[3,32,512]{2,1,0:T(8,128)S(1)}, u32[]{:S(2)}, u32[]{:S(2)}) %collective-permute-start.1) | collective-permute-done | bytes 196640 | tf_op jit(solution)/shard_map/ppermute | solution.py:97
  13.8 8.9 %collective-permute-done.2 = f32[2,3,32,512]{3,2,1,0:T(8,128)S(1)} collective-permute-done((f32[2,3,32,512]{3,2,1,0:T(8,128)S(1)}, f32[2,3,32,512]{3,2,1,0:T(8,128)S(1)}, u32[]{:S(2)}, u32[]{:S(2)}) %collective-permute-start.2) | collective-permute-done | bytes 393248 | tf_op jit(solution)/shard_map/ppermute | solution.py:97
  26.5 6.0 %all-to-all-start = ((f32[3,256,512]{2,0,1:T(4,128)}), f32[3,256,512]{2,0,1:T(4,128)S(1)}, u32[]{:S(2)}, u32[]{:S(2)}) async-start(f32[3,256,512]{2,0,1:T(4,128)} %bitcast.1), calls=%async_computation | async-start | bytes 4194304 | tf_op jit(solution)/shard_map/all_to_all | solution.py:112
  32.6 11.8 %collective-permute-done.3 = f32[2,2,3,32,512]{4,3,2,0,1:T(8,128)} collective-permute-done((f32[2,2,3,32,512]{4,3,2,0,1:T(8,128)}, f32[2,2,3,32,512]{4,3,2,0,1:T(8,128)}, u32[]{:S(2)}, u32[]{:S(2)}) %collective-permute-start.3) | collective-permute-done | bytes 786464 | tf_op jit(solution)/shard_map/ppermute | solution.py:97
  47.1 7.7 %fusion = f32[512,6,256,1]{0,2,3,1:T(8,128)S(1)} fusion(f32[3,256,512,1]{2,1,0,3:T(8,128)S(1)} %bitcast.185, f32[3,1,256,6,1,256]{5,4,3,2,1,0:T(1,128)S(1)} %bitcast.181), kind=kOutput, calls=%fused_computation | convolution fusion | flops 7247757312 | bytes 9437184 | tf_op jit(solution)/shard_map/lsmt,lsw->mtw/dot_general | solution.py:123
  57.6 6.6 %all-to-all-done = f32[3,256,512]{2,0,1:T(4,128)S(1)} async-done(((f32[3,256,512]{2,0,1:T(4,128)}), f32[3,256,512]{2,0,1:T(4,128)S(1)}, u32[]{:S(2)}, u32[]{:S(2)}) %all-to-all-start) | async-done | bytes 1572896 | tf_op jit(solution)/shard_map/all_to_all | solution.py:112
  64.2 10.4 %fusion.2 = f32[512,6,256,1]{0,2,3,1:T(8,128)S(1)} fusion(f32[3,1,256,6,1,256]{5,4,3,2,1,0:T(1,128)} %param.7, f32[3,256,512]{2,0,1:T(4,128)S(1)} %all-to-all-done), kind=kOutput, calls=%fused_computation.2 | convolution fusion | flops 7247757312 | bytes 9437184 | tf_op jit(solution)/shard_map/lsmt,lsw->mtw/dot_general | solution.py:123
  76.9 2.9 %bitcast_add_fusion = f32[3,8,32,512]{3,2,0,1:T(8,128)} fusion(f32[3,8,32,512]{3,2,0,1:T(8,128)} %collective-permute-done.4, f32[3,8,1,32,512]{4,3,2,1,0:T(8,128)S(1)} %copy-done), kind=kLoop, calls=%fused_computation.8 | loop fusion | flops 393216 | bytes 4718592 | tf_op jit(solution)/shard_map/add | solution.py:57
  79.8 7.4 %all-to-all-start.2 = ((f32[3,8,32,512]{3,2,0,1:T(8,128)}), f32[3,8,32,512]{3,2,0,1:T(8,128)S(1)}, u32[]{:S(2)}, u32[]{:S(2)}) async-start(f32[3,8,32,512]{3,2,0,1:T(8,128)} %bitcast_add_fusion), calls=%async_computation.2 | async-start | bytes 3145728 | tf_op jit(solution)/shard_map/all_to_all | solution.py:119
  87.3 2.9 %bitcast_add_fusion.1 = f32[3,8,32,512]{3,2,0,1:T(8,128)} fusion(f32[3,8,32,512]{3,2,0,1:T(8,128)} %collective-permute-done, f32[3,8,1,32,512]{4,3,2,1,0:T(8,128)S(1)} %get-tuple-element.8), kind=kLoop, calls=%fused_computation.9 | loop fusion | flops 393216 | bytes 4718592 | tf_op jit(solution)/shard_map/add | solution.py:57
  90.2 17.3 %all-to-all-done.2 = f32[3,8,32,512]{3,2,0,1:T(8,128)S(1)} async-done(((f32[3,8,32,512]{3,2,0,1:T(8,128)}), f32[3,8,32,512]{3,2,0,1:T(8,128)S(1)}, u32[]{:S(2)}, u32[]{:S(2)}) %all-to-all-start.2) | async-done | bytes 1572896 | tf_op jit(solution)/shard_map/all_to_all | solution.py:119
  107.4 6.2 %all-to-all-start.1 = ((f32[3,8,32,512]{3,2,0,1:T(8,128)}), f32[3,8,32,512]{3,2,0,1:T(8,128)S(1)}, u32[]{:S(2)}, u32[]{:S(2)}) async-start(f32[3,8,32,512]{3,2,0,1:T(8,128)} %bitcast_add_fusion.1), calls=%async_computation.1 | async-start | bytes 3145728 | tf_op jit(solution)/shard_map/all_to_all | solution.py:119
  114.5 5.5 %collective-permute-start.6 = (f32[3,32,1024]{2,1,0:T(8,128)}, f32[3,32,1024]{2,1,0:T(8,128)}, u32[]{:S(2)}, u32[]{:S(2)}) collective-permute-start(f32[3,32,1024]{2,1,0:T(8,128)} %pad_maximum_fusion.2), channel_id=1, source_target_pairs={{0,0},{1,8},{2,16},{3,24},{4,32},{5,40},{6,48},{7,56},{8,1},{9,9},... | collective-permute-start | bytes 1179656 | tf_op jit(solution)/shard_map/ppermute | solution.py:81
  120.1 13.1 %all-to-all-done.1 = f32[3,8,32,512]{3,2,0,1:T(8,128)S(1)} async-done(((f32[3,8,32,512]{3,2,0,1:T(8,128)}), f32[3,8,32,512]{3,2,0,1:T(8,128)S(1)}, u32[]{:S(2)}, u32[]{:S(2)}) %all-to-all-start.1) | async-done | bytes 1572896 | tf_op jit(solution)/shard_map/all_to_all | solution.py:119
  133.5 17.5 %collective-permute-done.6 = f32[3,32,1024]{2,1,0:T(8,128)} collective-permute-done((f32[3,32,1024]{2,1,0:T(8,128)}, f32[3,32,1024]{2,1,0:T(8,128)}, u32[]{:S(2)}, u32[]{:S(2)}) %collective-permute-start.6) | collective-permute-done | bytes 393248 | tf_op jit(solution)/shard_map/ppermute | solution.py:81
  151.0 2.0 convolution_bitcast_fusion
  152.9 2.0 convolution_bitcast_fusion.1
  157.3 2.1 collective-permute-done.7
  159.9 20.2 %all_to_all.33 = f32[64,1,2560]{2,1,0:T(1,128)S(1)} all-to-all(f32[64,1,2560]{2,1,0:T(1,128)S(1)} %all_to_all.24), channel_id=1, replica_groups=mesh['prow_hi'=8,'core'=2,'pcol'=8] {'prow_hi','pcol'}, dimensions={0} | all-to-all | bytes 1310720 | tf_op jit(solution)/shard_map/all_to_all | solution.py:173
  180.8 18.1 %all_to_all.34 = f32[64,1,2560]{2,1,0:T(1,128)S(1)} all-to-all(f32[64,1,2560]{2,1,0:T(1,128)S(1)} %broadcast_in_dim.28), channel_id=1, replica_groups=mesh['prow_hi'=8,'core'=2,'pcol'=8] {'prow_hi','pcol'}, dimensions={0} | all-to-all | bytes 1310720 | tf_op jit(solution)/shard_map/all_to_all | solution.py:175
  199.1 5.1 %collective-permute-start.5 = (f32[3,32,1024]{2,1,0:T(8,128)S(1)}, f32[3,32,1024]{2,1,0:T(8,128)S(1)}, u32[]{:S(2)}, u32[]{:S(2)}) collective-permute-start(f32[3,32,1024]{2,1,0:T(8,128)S(1)} %pad_maximum_fusion.1), channel_id=1, source_target_pairs={{0,0},{8,1},{16,2},{24,3},{32,4},{40,5},{48,6},{56,7},{1,8},{9,9},... | collective-permute-start | bytes 1179656 | tf_op jit(solution)/shard_map/ppermute | solution.py:167
  204.2 19.4 %collective-permute-done.5 = f32[3,32,1024]{2,1,0:T(8,128)S(1)} collective-permute-done((f32[3,32,1024]{2,1,0:T(8,128)S(1)}, f32[3,32,1024]{2,1,0:T(8,128)S(1)}, u32[]{:S(2)}, u32[]{:S(2)}) %collective-permute-start.5) | collective-permute-done | bytes 393248 | tf_op jit(solution)/shard_map/ppermute | solution.py:167
  224.9 1.9 maximum_select_fusion.1
  (91 shorter events, 28.4 us)
Async XLA Ops:
  0.6 13.1 %copy-start.1 = (f32[3,1,32,512]{3,2,1,0:T(8,128)S(1)}, f32[3,1,32,512]{3,2,1,0:T(8,128)}, u32[]{:S(2)}) copy-start(f32[3,1,32,512]{3,2,1,0:T(8,128)} %param.9) | copy-start | bytes 589828
  3.4 8.9 %copy-start.6 = (f32[3,32,512]{2,1,0:T(8,128)}, f32[3,32,512]{2,1,0:T(8,128)S(1)}, u32[]{:S(2)}) copy-start(f32[3,32,512]{2,1,0:T(8,128)S(1)} %bitcast_multiply_fusion.1) | copy-start | bytes 589828
  3.4 8.9 %collective-permute-start.1 = (f32[3,32,512]{2,1,0:T(8,128)S(1)}, f32[3,32,512]{2,1,0:T(8,128)S(1)}, u32[]{:S(2)}, u32[]{:S(2)}) collective-permute-start(f32[3,32,512]{2,1,0:T(8,128)S(1)} %bitcast_multiply_fusion.1), channel_id=1, source_target_pairs={{0,2},{1,3},{2,0},{3,1},{4,6},{5,7},{6,4},{7,5},{8,10},{9,11},{10,... | collective-permute-start | bytes 589832 | tf_op jit(solution)/shard_map/ppermute | solution.py:97
  12.3 12.2 %copy-start.4 = (f32[3,1,32,512]{3,2,1,0:T(8,128)S(1)}, f32[3,1,32,512]{3,2,1,0:T(8,128)}, u32[]{:S(2)}) copy-start(f32[3,1,32,512]{3,2,1,0:T(8,128)} %param.8) | copy-start | bytes 589828
  12.4 10.4 %collective-permute-start.2 = (f32[2,3,32,512]{3,2,1,0:T(8,128)S(1)}, f32[2,3,32,512]{3,2,1,0:T(8,128)S(1)}, u32[]{:S(2)}, u32[]{:S(2)}) collective-permute-start(f32[2,3,32,512]{3,2,1,0:T(8,128)S(1)} %maximum_select_fusion.5), channel_id=1, source_target_pairs={{0,1},{1,0},{2,3},{3,2},{4,5},{5,4},{6,7},{7,6},{8,9},{9,8},{10,11... | collective-permute-start | bytes 1179656 | tf_op jit(solution)/shard_map/ppermute | solution.py:97
  23.7 20.7 %collective-permute-start.3 = (f32[2,2,3,32,512]{4,3,2,0,1:T(8,128)}, f32[2,2,3,32,512]{4,3,2,0,1:T(8,128)}, u32[]{:S(2)}, u32[]{:S(2)}) collective-permute-start(f32[2,2,3,32,512]{4,3,2,0,1:T(8,128)} %maximum_select_fusion.3), channel_id=1, source_target_pairs={{0,4},{1,5},{2,6},{3,7},{4,0},{5,1},{6,2},{7,3},{8,12},{9,13},{10,... | collective-permute-start | bytes 2359304 | tf_op jit(solution)/shard_map/ppermute | solution.py:97
  26.5 20.0 %slice-start = ((s8[4718592]{0:T(1024)(128)(4,1)}), s8[524288]{0:T(1024)(128)(4,1)S(1)}, s32[]{:S(2)}) async-start(s8[4718592]{0:T(1024)(128)(4,1)} %bitcast.180), calls=%async_computation.5 | async-start | bytes 1048576
  26.5 37.7 %all-to-all-start = ((f32[3,256,512]{2,0,1:T(4,128)}), f32[3,256,512]{2,0,1:T(4,128)S(1)}, u32[]{:S(2)}, u32[]{:S(2)}) async-start(f32[3,256,512]{2,0,1:T(4,128)} %bitcast.1), calls=%async_computation | async-start | bytes 4194304 | tf_op jit(solution)/shard_map/all_to_all | solution.py:112
  44.4 2.7 %slice-start.1 = ((s8[4718592]{0:T(1024)(128)(4,1)}), s8[4194304]{0:T(1024)(128)(4,1)S(1)}, s32[]{:S(2)}) async-start(s8[4718592]{0:T(1024)(128)(4,1)} %bitcast.180), calls=%async_computation.6 | async-start | bytes 8388608
  57.6 18.7 %collective-permute-start.4 = (f32[3,8,32,512]{3,2,0,1:T(8,128)}, f32[3,8,32,512]{3,2,0,1:T(8,128)}, u32[]{:S(2)}, u32[]{:S(2)}) collective-permute-start(f32[3,8,32,512]{3,2,0,1:T(8,128)} %bitcast.176), channel_id=1, source_target_pairs={{0,8},{8,0},{1,9},{9,1},{2,10},{10,2},{3,11},{11,3},{4,12},{12,4},... | collective-permute-start | bytes 4718600 | tf_op jit(solution)/shard_map/ppermute | solution.py:57
  74.9 2.0 copy-start
  76.2 11.0 %collective-permute-start = (f32[3,8,32,512]{3,2,0,1:T(8,128)}, f32[3,8,32,512]{3,2,0,1:T(8,128)}, u32[]{:S(2)}, u32[]{:S(2)}) collective-permute-start(f32[3,8,32,512]{3,2,0,1:T(8,128)} %bitcast.177), channel_id=1, source_target_pairs={{0,8},{8,0},{1,9},{9,1},{2,10},{10,2},{3,11},{11,3},{4,12},{12,4},... | collective-permute-start | bytes 4718600 | tf_op jit(solution)/shard_map/ppermute | solution.py:57
  79.8 27.6 %all-to-all-start.2 = ((f32[3,8,32,512]{3,2,0,1:T(8,128)}), f32[3,8,32,512]{3,2,0,1:T(8,128)S(1)}, u32[]{:S(2)}, u32[]{:S(2)}) async-start(f32[3,8,32,512]{3,2,0,1:T(8,128)} %bitcast_add_fusion), calls=%async_computation.2 | async-start | bytes 3145728 | tf_op jit(solution)/shard_map/all_to_all | solution.py:119
  90.2 23.5 %copy-start.5 = (f32[3,1,32,512]{3,2,1,0:T(8,128)S(1)}, f32[3,1,32,512]{3,2,1,0:T(8,128)}, u32[]{:S(2)}) copy-start(f32[3,1,32,512]{3,2,1,0:T(8,128)} %param.8) | copy-start | bytes 589828
  90.2 23.6 %copy-start.7 = (f32[3,32,512]{2,1,0:T(8,128)S(1)}, f32[3,32,512]{2,1,0:T(8,128)}, u32[]{:S(2)}) copy-start(f32[3,32,512]{2,1,0:T(8,128)} %copy-done.6) | copy-start | bytes 589828
  107.4 25.7 %all-to-all-start.1 = ((f32[3,8,32,512]{3,2,0,1:T(8,128)}), f32[3,8,32,512]{3,2,0,1:T(8,128)S(1)}, u32[]{:S(2)}, u32[]{:S(2)}) async-start(f32[3,8,32,512]{3,2,0,1:T(8,128)} %bitcast_add_fusion.1), calls=%async_computation.1 | async-start | bytes 3145728 | tf_op jit(solution)/shard_map/all_to_all | solution.py:119
  114.5 36.5 %collective-permute-start.6 = (f32[3,32,1024]{2,1,0:T(8,128)}, f32[3,32,1024]{2,1,0:T(8,128)}, u32[]{:S(2)}, u32[]{:S(2)}) collective-permute-start(f32[3,32,1024]{2,1,0:T(8,128)} %pad_maximum_fusion.2), channel_id=1, source_target_pairs={{0,0},{1,8},{2,16},{3,24},{4,32},{5,40},{6,48},{7,56},{8,1},{9,9},... | collective-permute-start | bytes 1179656 | tf_op jit(solution)/shard_map/ppermute | solution.py:81
  157.2 2.2 collective-permute-start.7
  199.0 25.4 %collective-permute-start.8 = (f32[64,2560]{1,0:T(8,128)S(1)}, f32[64,2560]{1,0:T(8,128)S(1)}, u32[]{:S(2)}, u32[]{:S(2)}) collective-permute-start(f32[64,2560]{1,0:T(8,128)S(1)} %bitcast.195), channel_id=1, source_target_pairs={{0,8},{8,0},{1,9},{9,1},{2,10},{10,2},{3,11},{11,3},{4,12},{12,4},... | collective-permute-start | bytes 1966088 | tf_op jit(solution)/shard_map/ppermute | solution.py:176
  199.1 24.5 %collective-permute-start.5 = (f32[3,32,1024]{2,1,0:T(8,128)S(1)}, f32[3,32,1024]{2,1,0:T(8,128)S(1)}, u32[]{:S(2)}, u32[]{:S(2)}) collective-permute-start(f32[3,32,1024]{2,1,0:T(8,128)S(1)} %pad_maximum_fusion.1), channel_id=1, source_target_pairs={{0,0},{8,1},{16,2},{24,3},{32,4},{40,5},{48,6},{56,7},{1,8},{9,9},... | collective-permute-start | bytes 1179656 | tf_op jit(solution)/shard_map/ppermute | solution.py:167
  228.9 1.2 copy-start.2
  228.9 1.5 copy-start.3
where the time goes:
time: 234 us; the launch traced here: 232 us
  waiting for transfers between devices  100 us (43%)
  blocking collectives  38.3 us (16%)
  starting transfers between devices  36.5 us (16%)
  matrix products  22 us (9%)
  other arithmetic  17.1 us (7%)
  local copies, waits for them, and re-layouts  16.7 us (7%)
    all_to_all x2, waiting for transfers between devices, reduce_gathered(): received = lax.all_to_all(pre, 'prow_hi', 1, 1, tiled=True)  30.3 us
    ppermute x3, waiting for transfers between devices, gather_piece(): lax.ppermute(held, 'pcol', [(i, i ^ 1 << b) for i in range(col_count)])  24.6 us
    all_to_all x1, blocking collectives, body(): reduced = jnp.sum(lax.all_to_all(flat, others, 0, 0, tiled=True), axis=0)  20.2 us
    ppermute x1, waiting for transfers between devices, body(): column_home = lax.ppermute(column, both, to_owner)  19.4 us
    all_to_all x1, blocking collectives, body(): lax.all_to_all(spread_sum, others, 0, 0, tiled=True).reshape(half.shape)  18.1 us
    dot_general x2, matrix products, product_of(): jnp.einsum('lsmt,lsw->mtw', matrix, gathered, precision=highest, preferre...  18.1 us
    ppermute x1, waiting for transfers between devices, body(): x_at_reducer = lax.ppermute(x, both, to_reducer)  17.5 us
    all_to_all x2, starting transfers between devices, reduce_gathered(): received = lax.all_to_all(pre, 'prow_hi', 1, 1, tiled=True)  13.6 us
  transfers between devices with their start and end apart: 12, of which 9 were waited for; matrix products, arithmetic and copies ran while one was open for 15% of the time, Pallas kernels for 0%

commit v1 on v0

--- a/solution.py
+++ b/solution.py
@@ -84,7 +84,7 @@
 
     def reduce_inner(piece, by_permutes):
         gathered = gather_piece(piece, by_permutes)
-        return reduce_gathered(piece, gathered)
+        return reduce_gathered(piece, gathered, by_permutes)
 
     def gather_piece(piece, by_permutes):
         if by_permutes:
@@ -112,12 +112,26 @@
             gathered = lax.all_to_all(spread, "pcol", 1, 1, tiled=True)
         return gathered
 
-    def reduce_gathered(piece, gathered):
+    def reduce_gathered(piece, gathered, by_permutes):
         partial = product_of(gathered)
         chunks = partial.reshape(row_blocks, row_count, slice_rows, piece.shape[-1])
         pre = pair_sum(chunks, 1)
+        if by_permutes:
+            return halve_over_prow(pre)
         received = lax.all_to_all(pre, "prow_hi", 1, 1, tiled=True)
         return jnp.sum(received, axis=1)
+
+    def halve_over_prow(pre):
+        size = lax.axis_size("prow_hi")
+        bits = size.bit_length() - 1
+        me = lax.axis_index("prow_hi")
+        held = pre.reshape(pre.shape[:1] + (2,) * bits + pre.shape[2:])
+        for b in reversed(range(bits)):
+            mine = (me >> b) & 1
+            keep = lax.dynamic_index_in_dim(held, mine, 1, False)
+            send = lax.dynamic_index_in_dim(held, 1 - mine, 1, False)
+            held = keep + lax.ppermute(send, "prow_hi", [(i, i ^ (1 << b)) for i in range(size)])
+        return held
 
     def product_of(gathered):
         return jnp.einsum(
@@ -129,10 +143,7 @@
         )
 
     total = jnp.concatenate(
-        [
-            reduce_inner(x[..., k * PIECE:(k + 1) * PIECE], k > 0)
-            for k in range(2 * width // PIECE)
-        ],
+        [reduce_inner(x[..., k * PIECE:(k + 1) * PIECE], k > 0) for k in range(2 * width // PIECE)],
         axis=-1,
     )
 

time: 234 us -> 235 us (level)
  waiting for transfers between devices: 100 us -> 83.3 us
  starting transfers between devices: 36.5 us -> 50.2 us
  blocking collectives: 38.3 us -> 41.3 us
    all_to_all x2 -> x1, waiting for transfers between devices: 30.3 us -> 0.01 us  [reduce_gathered(): received = lax.all_to_all(pre, 'prow_hi', 1, 1, tiled=True)]
    ppermute x0 -> x3, waiting for transfers between devices: none -> 30 us  [halve_over_prow(): lax.ppermute(send, 'prow_hi', [(i, i ^ 1 << b) for i in range(size)])]
    ppermute x0 -> x3, starting transfers between devices: none -> 23.3 us  [halve_over_prow(): lax.ppermute(send, 'prow_hi', [(i, i ^ 1 << b) for i in range(size)])]
    ppermute x1, waiting for transfers between devices: 17.5 us -> 0.01 us  [body(): x_at_reducer = lax.ppermute(x, both, to_reducer)]
    all_to_all x2 -> x1, starting transfers between devices: 13.6 us -> 5.49 us  [reduce_gathered(): received = lax.all_to_all(pre, 'prow_hi', 1, 1, tiled=True)]
    all_to_all x1, blocking collectives: 20.2 us -> 23.2 us  [body(): reduced = jnp.sum(lax.all_to_all(flat, others, 0, 0, tiled=True), axis=0)]
  transfers between devices with their start and end apart: 12 -> 14, of which waited for: 9 -> 9; matrix products, arithmetic and copies ran while one was open for 15% -> 15% of each run, Pallas kernels for 0% -> 0%
where the time goes in v1:
time: 235 us; the launch traced here: 233 us
  waiting for transfers between devices  83.3 us (35%)
  starting transfers between devices  50.2 us (21%)
  blocking collectives  41.3 us (18%)
  matrix products  22 us (9%)
  local copies, waits for them, and re-layouts  18 us (8%)
  other arithmetic  17.2 us (7%)
    ppermute x3, waiting for transfers between devices, halve_over_prow(): lax.ppermute(send, 'prow_hi', [(i, i ^ 1 << b) for i in range(size)])  30 us
    ppermute x3, waiting for transfers between devices, gather_piece(): lax.ppermute(held, 'pcol', [(i, i ^ 1 << b) for i in range(col_count)])  24.6 us
    ppermute x3, starting transfers between devices, halve_over_prow(): lax.ppermute(send, 'prow_hi', [(i, i ^ 1 << b) for i in range(size)])  23.3 us
    all_to_all x1, blocking collectives, body(): reduced = jnp.sum(lax.all_to_all(flat, others, 0, 0, tiled=True), axis=0)  23.2 us
    ppermute x1, waiting for transfers between devices, body(): column_home = lax.ppermute(column, both, to_owner)  19.4 us
    all_to_all x1, blocking collectives, body(): lax.all_to_all(spread_sum, others, 0, 0, tiled=True).reshape(half.shape)  18.1 us
    dot_general x2, matrix products, product_of(): jnp.einsum('lsmt,lsw->mtw', matrix, gathered, precision=highest, preferre...  18.1 us
    all_to_all x1, waiting for transfers between devices, gather_piece(): gathered = lax.all_to_all(spread, 'pcol', 1, 1, tiled=True)  7.21 us
  transfers between devices with their start and end apart: 14, of which 9 were waited for; matrix products, arithmetic and copies ran while one was open for 15% of the time, Pallas kernels for 0%

profile of v1, /device:TPU:6, one launch (start us, length us, event | category | flops | bytes accessed | tf_op | source)
XLA Modules:
  0.0 233.3 jit_solution(4553679800603454236)
XLA Ops:
  3.4 4.0 %collective-permute-start.1 = (f32[3,32,512]{2,1,0:T(8,128)S(1)}, f32[3,32,512]{2,1,0:T(8,128)S(1)}, u32[]{:S(2)}, u32[]{:S(2)}) collective-permute-start(f32[3,32,512]{2,1,0:T(8,128)S(1)} %bitcast_multiply_fusion.1), channel_id=1, source_target_pairs={{0,2},{1,3},{2,0},{3,1},{4,6},{5,7},{6,4},{7,5},{8,10},{9,11},{10,... | collective-permute-start | bytes 589832 | tf_op jit(solution)/shard_map/ppermute | solution.py:97
  8.4 3.9 %collective-permute-done.1 = f32[3,32,512]{2,1,0:T(8,128)S(1)} collective-permute-done((f32[3,32,512]{2,1,0:T(8,128)S(1)}, f32[3,32,512]{2,1,0:T(8,128)S(1)}, u32[]{:S(2)}, u32[]{:S(2)}) %collective-permute-start.1) | collective-permute-done | bytes 196640 | tf_op jit(solution)/shard_map/ppermute | solution.py:97
  13.8 8.9 %collective-permute-done.2 = f32[2,3,32,512]{3,2,1,0:T(8,128)S(1)} collective-permute-done((f32[2,3,32,512]{3,2,1,0:T(8,128)S(1)}, f32[2,3,32,512]{3,2,1,0:T(8,128)S(1)}, u32[]{:S(2)}, u32[]{:S(2)}) %collective-permute-start.2) | collective-permute-done | bytes 393248 | tf_op jit(solution)/shard_map/ppermute | solution.py:97
  26.5 6.0 %all-to-all-start = ((f32[3,256,512]{2,0,1:T(4,128)}), f32[3,256,512]{2,0,1:T(4,128)S(1)}, u32[]{:S(2)}, u32[]{:S(2)}) async-start(f32[3,256,512]{2,0,1:T(4,128)} %bitcast.1), calls=%async_computation | async-start | bytes 4194304 | tf_op jit(solution)/shard_map/all_to_all | solution.py:112
  32.6 11.8 %collective-permute-done.3 = f32[2,2,3,32,512]{4,3,2,0,1:T(8,128)} collective-permute-done((f32[2,2,3,32,512]{4,3,2,0,1:T(8,128)}, f32[2,2,3,32,512]{4,3,2,0,1:T(8,128)}, u32[]{:S(2)}, u32[]{:S(2)}) %collective-permute-start.3) | collective-permute-done | bytes 786464 | tf_op jit(solution)/shard_map/ppermute | solution.py:97
  47.1 7.7 %fusion = f32[512,6,256,1]{0,2,3,1:T(8,128)S(1)} fusion(f32[3,256,512,1]{2,1,0,3:T(8,128)S(1)} %bitcast.204, f32[3,1,256,6,1,256]{5,4,3,2,1,0:T(1,128)S(1)} %bitcast.198), kind=kOutput, calls=%fused_computation | convolution fusion | flops 7247757312 | bytes 9437184 | tf_op jit(solution)/shard_map/lsmt,lsw->mtw/dot_general | solution.py:137
  57.0 7.2 %all-to-all-done = f32[3,256,512]{2,0,1:T(4,128)S(1)} async-done(((f32[3,256,512]{2,0,1:T(4,128)}), f32[3,256,512]{2,0,1:T(4,128)S(1)}, u32[]{:S(2)}, u32[]{:S(2)}) %all-to-all-start) | async-done | bytes 1572896 | tf_op jit(solution)/shard_map/all_to_all | solution.py:112
  64.2 10.4 %fusion.2 = f32[512,6,256,1]{0,2,3,1:T(8,128)S(1)} fusion(f32[3,1,256,6,1,256]{5,4,3,2,1,0:T(1,128)} %param.7, f32[3,256,512]{2,0,1:T(4,128)S(1)} %all-to-all-done), kind=kOutput, calls=%fused_computation.2 | convolution fusion | flops 7247757312 | bytes 9437184 | tf_op jit(solution)/shard_map/lsmt,lsw->mtw/dot_general | solution.py:137
  80.5 3.3 %collective-permute-start.5 = (f32[3,2,2,32,512]{4,3,0,2,1:T(8,128)S(1)}, f32[3,2,2,32,512]{4,3,0,2,1:T(8,128)}, u32[]{:S(2)}, u32[]{:S(2)}) collective-permute-start(f32[3,2,2,32,512]{4,3,0,2,1:T(8,128)S(1)} %bitcast.214), channel_id=1, source_target_pairs={{0,64},{16,80},{32,96},{48,112},{64,0},{80,16},{96,32},{112,48},{1... | collective-permute-start | bytes 2359304 | tf_op jit(solution)/shard_map/ppermute | solution.py:133
  83.8 3.0 %bitcast_add_fusion.1 = f32[3,8,32,512]{3,2,0,1:T(8,128)} fusion(f32[3,8,32,512]{3,2,0,1:T(8,128)} %collective-permute-done, f32[3,8,1,32,512]{4,3,2,1,0:T(8,128)S(1)} %copy-done.2), kind=kLoop, calls=%fused_computation.9 | loop fusion | flops 393216 | bytes 4718592 | tf_op jit(solution)/shard_map/add | solution.py:57
  86.8 5.5 %all-to-all-start.1 = ((f32[3,8,32,512]{3,2,0,1:T(8,128)}), f32[3,8,32,512]{3,2,0,1:T(8,128)S(1)}, u32[]{:S(2)}, u32[]{:S(2)}) async-start(f32[3,8,32,512]{3,2,0,1:T(8,128)} %bitcast_add_fusion.1), calls=%async_computation.1 | async-start | bytes 3145728 | tf_op jit(solution)/shard_map/all_to_all | solution.py:121
  92.3 18.9 %collective-permute-done.5 = f32[3,2,2,32,512]{4,3,0,2,1:T(8,128)} collective-permute-done((f32[3,2,2,32,512]{4,3,0,2,1:T(8,128)S(1)}, f32[3,2,2,32,512]{4,3,0,2,1:T(8,128)}, u32[]{:S(2)}, u32[]{:S(2)}) %collective-permute-start.5) | collective-permute-done | bytes 786464 | tf_op jit(solution)/shard_map/ppermute | solution.py:133
  115.0 3.9 %collective-permute-start.9 = (f32[3,32,1024]{2,1,0:T(8,128)}, f32[3,32,1024]{2,1,0:T(8,128)}, u32[]{:S(2)}, u32[]{:S(2)}) collective-permute-start(f32[3,32,1024]{2,1,0:T(8,128)} %pad_maximum_fusion.2), channel_id=1, source_target_pairs={{0,0},{1,8},{2,16},{3,24},{4,32},{5,40},{6,48},{7,56},{8,1},{9,9},... | collective-permute-start | bytes 1179656 | tf_op jit(solution)/shard_map/ppermute | solution.py:81
  118.9 7.7 %collective-permute-done.6 = f32[3,2,32,512]{3,2,0,1:T(8,128)S(1)} collective-permute-done((f32[3,2,32,512]{3,2,0,1:T(8,128)S(1)}, f32[3,2,32,512]{3,2,0,1:T(8,128)S(1)}, u32[]{:S(2)}, u32[]{:S(2)}) %collective-permute-start.6) | collective-permute-done | bytes 393248 | tf_op jit(solution)/shard_map/ppermute | solution.py:133
  126.7 18.3 %collective-permute-start.7 = (f32[3,32,512]{2,1,0:T(8,128)S(1)}, f32[3,32,512]{2,1,0:T(8,128)S(1)}, u32[]{:S(2)}, u32[]{:S(2)}) collective-permute-start(f32[3,32,512]{2,1,0:T(8,128)S(1)} %dynamic-slice_bitcast_fusion.2), channel_id=1, source_target_pairs={{0,16},{16,0},{32,48},{48,32},{64,80},{80,64},{96,112},{112,96},{1... | collective-permute-start | bytes 589832 | tf_op jit(solution)/shard_map/ppermute | solution.py:133
  145.2 3.4 %collective-permute-done.7 = f32[3,32,512]{2,1,0:T(8,128)S(1)} collective-permute-done((f32[3,32,512]{2,1,0:T(8,128)S(1)}, f32[3,32,512]{2,1,0:T(8,128)S(1)}, u32[]{:S(2)}, u32[]{:S(2)}) %collective-permute-start.7) | collective-permute-done | bytes 196640 | tf_op jit(solution)/shard_map/ppermute | solution.py:133
  148.8 2.0 convolution_bitcast_fusion
  150.7 2.0 convolution_bitcast_fusion.1
  155.3 2.1 collective-permute-done.10
  157.9 23.2 %all_to_all.28 = f32[64,1,2560]{2,1,0:T(1,128)S(1)} all-to-all(f32[64,1,2560]{2,1,0:T(1,128)S(1)} %all_to_all.20), channel_id=1, replica_groups=mesh['prow_hi'=8,'core'=2,'pcol'=8] {'prow_hi','pcol'}, dimensions={0} | all-to-all | bytes 1310720 | tf_op jit(solution)/shard_map/all_to_all | solution.py:184
  181.8 18.1 %all_to_all.29 = f32[64,1,2560]{2,1,0:T(1,128)S(1)} all-to-all(f32[64,1,2560]{2,1,0:T(1,128)S(1)} %broadcast_in_dim.28), channel_id=1, replica_groups=mesh['prow_hi'=8,'core'=2,'pcol'=8] {'prow_hi','pcol'}, dimensions={0} | all-to-all | bytes 1310720 | tf_op jit(solution)/shard_map/all_to_all | solution.py:186
  200.1 5.1 %collective-permute-start.8 = (f32[3,32,1024]{2,1,0:T(8,128)S(1)}, f32[3,32,1024]{2,1,0:T(8,128)S(1)}, u32[]{:S(2)}, u32[]{:S(2)}) collective-permute-start(f32[3,32,1024]{2,1,0:T(8,128)S(1)} %pad_maximum_fusion.1), channel_id=1, source_target_pairs={{0,0},{8,1},{16,2},{24,3},{32,4},{40,5},{48,6},{56,7},{1,8},{9,9},... | collective-permute-start | bytes 1179656 | tf_op jit(solution)/shard_map/ppermute | solution.py:178
  205.3 19.4 %collective-permute-done.8 = f32[3,32,1024]{2,1,0:T(8,128)S(1)} collective-permute-done((f32[3,32,1024]{2,1,0:T(8,128)S(1)}, f32[3,32,1024]{2,1,0:T(8,128)S(1)}, u32[]{:S(2)}, u32[]{:S(2)}) %collective-permute-start.8) | collective-permute-done | bytes 393248 | tf_op jit(solution)/shard_map/ppermute | solution.py:178
  225.9 1.9 maximum_select_fusion.1
  (103 shorter events, 34.6 us)
Async XLA Ops:
  0.6 13.1 %copy-start.3 = (f32[3,1,32,512]{3,2,1,0:T(8,128)S(1)}, f32[3,1,32,512]{3,2,1,0:T(8,128)}, u32[]{:S(2)}) copy-start(f32[3,1,32,512]{3,2,1,0:T(8,128)} %param.9) | copy-start | bytes 589828
  3.4 8.9 %copy-start.8 = (f32[3,32,512]{2,1,0:T(8,128)}, f32[3,32,512]{2,1,0:T(8,128)S(1)}, u32[]{:S(2)}) copy-start(f32[3,32,512]{2,1,0:T(8,128)S(1)} %bitcast_multiply_fusion.1) | copy-start | bytes 589828
  3.4 8.9 %collective-permute-start.1 = (f32[3,32,512]{2,1,0:T(8,128)S(1)}, f32[3,32,512]{2,1,0:T(8,128)S(1)}, u32[]{:S(2)}, u32[]{:S(2)}) collective-permute-start(f32[3,32,512]{2,1,0:T(8,128)S(1)} %bitcast_multiply_fusion.1), channel_id=1, source_target_pairs={{0,2},{1,3},{2,0},{3,1},{4,6},{5,7},{6,4},{7,5},{8,10},{9,11},{10,... | collective-permute-start | bytes 589832 | tf_op jit(solution)/shard_map/ppermute | solution.py:97
  12.3 12.2 %copy-start.6 = (f32[3,1,32,512]{3,2,1,0:T(8,128)S(1)}, f32[3,1,32,512]{3,2,1,0:T(8,128)}, u32[]{:S(2)}) copy-start(f32[3,1,32,512]{3,2,1,0:T(8,128)} %param.8) | copy-start | bytes 589828
  12.4 10.4 %collective-permute-start.2 = (f32[2,3,32,512]{3,2,1,0:T(8,128)S(1)}, f32[2,3,32,512]{3,2,1,0:T(8,128)S(1)}, u32[]{:S(2)}, u32[]{:S(2)}) collective-permute-start(f32[2,3,32,512]{3,2,1,0:T(8,128)S(1)} %maximum_select_fusion.5), channel_id=1, source_target_pairs={{0,1},{1,0},{2,3},{3,2},{4,5},{5,4},{6,7},{7,6},{8,9},{9,8},{10,11... | collective-permute-start | bytes 1179656 | tf_op jit(solution)/shard_map/ppermute | solution.py:97
  23.7 20.7 %collective-permute-start.3 = (f32[2,2,3,32,512]{4,3,2,0,1:T(8,128)}, f32[2,2,3,32,512]{4,3,2,0,1:T(8,128)}, u32[]{:S(2)}, u32[]{:S(2)}) collective-permute-start(f32[2,2,3,32,512]{4,3,2,0,1:T(8,128)} %maximum_select_fusion.3), channel_id=1, source_target_pairs={{0,4},{1,5},{2,6},{3,7},{4,0},{5,1},{6,2},{7,3},{8,12},{9,13},{10,... | collective-permute-start | bytes 2359304 | tf_op jit(solution)/shard_map/ppermute | solution.py:97
  26.5 20.0 %slice-start = ((s8[4718592]{0:T(1024)(128)(4,1)}), s8[524288]{0:T(1024)(128)(4,1)S(1)}, s32[]{:S(2)}) async-start(s8[4718592]{0:T(1024)(128)(4,1)} %bitcast.197), calls=%async_computation.4 | async-start | bytes 1048576
  26.5 37.8 %all-to-all-start = ((f32[3,256,512]{2,0,1:T(4,128)}), f32[3,256,512]{2,0,1:T(4,128)S(1)}, u32[]{:S(2)}, u32[]{:S(2)}) async-start(f32[3,256,512]{2,0,1:T(4,128)} %bitcast.1), calls=%async_computation | async-start | bytes 4194304 | tf_op jit(solution)/shard_map/all_to_all | solution.py:112
  44.4 2.7 %slice-start.1 = ((s8[4718592]{0:T(1024)(128)(4,1)}), s8[4194304]{0:T(1024)(128)(4,1)S(1)}, s32[]{:S(2)}) async-start(s8[4718592]{0:T(1024)(128)(4,1)} %bitcast.197), calls=%async_computation.5 | async-start | bytes 8388608
  54.8 2.2 copy-start
  57.0 20.4 %collective-permute-start.4 = (f32[3,8,32,512]{3,2,1,0:T(8,128)}, f32[3,8,32,512]{3,2,1,0:T(8,128)}, u32[]{:S(2)}, u32[]{:S(2)}) collective-permute-start(f32[3,8,32,512]{3,2,1,0:T(8,128)} %dynamic-slice_bitcast_fusion), channel_id=1, source_target_pairs={{0,8},{8,0},{1,9},{9,1},{2,10},{10,2},{3,11},{11,3},{4,12},{12,4},... | collective-permute-start | bytes 4718600 | tf_op jit(solution)/shard_map/ppermute | solution.py:57
  76.1 2.5 %copy-start.1 = (f32[512,6,256,1]{0,2,3,1:T(8,128)S(1)}, f32[512,6,256,1]{0,2,3,1:T(8,128)}, u32[]{:S(2)}) copy-start(f32[512,6,256,1]{0,2,3,1:T(8,128)} %copy-done) | copy-start | bytes 9437188
  77.4 6.4 %collective-permute-start = (f32[3,8,32,512]{3,2,0,1:T(8,128)}, f32[3,8,32,512]{3,2,0,1:T(8,128)}, u32[]{:S(2)}, u32[]{:S(2)}) collective-permute-start(f32[3,8,32,512]{3,2,0,1:T(8,128)} %bitcast.193), channel_id=1, source_target_pairs={{0,8},{8,0},{1,9},{9,1},{2,10},{10,2},{3,11},{11,3},{4,12},{12,4},... | collective-permute-start | bytes 4718600 | tf_op jit(solution)/shard_map/ppermute | solution.py:57
  80.5 3.3 %copy-start.2 = (f32[3,8,1,32,512]{4,3,2,1,0:T(8,128)S(1)}, f32[3,8,1,32,512]{4,3,2,1,0:T(8,128)}, u32[]{:S(2)}) copy-start(f32[3,8,1,32,512]{4,3,2,1,0:T(8,128)} %get-tuple-element.8) | copy-start | bytes 4718596
  80.5 30.6 %collective-permute-start.5 = (f32[3,2,2,32,512]{4,3,0,2,1:T(8,128)S(1)}, f32[3,2,2,32,512]{4,3,0,2,1:T(8,128)}, u32[]{:S(2)}, u32[]{:S(2)}) collective-permute-start(f32[3,2,2,32,512]{4,3,0,2,1:T(8,128)S(1)} %bitcast.214), channel_id=1, source_target_pairs={{0,64},{16,80},{32,96},{48,112},{64,0},{80,16},{96,32},{112,48},{1... | collective-permute-start | bytes 2359304 | tf_op jit(solution)/shard_map/ppermute | solution.py:133
  86.8 58.2 %all-to-all-start.1 = ((f32[3,8,32,512]{3,2,0,1:T(8,128)}), f32[3,8,32,512]{3,2,0,1:T(8,128)S(1)}, u32[]{:S(2)}, u32[]{:S(2)}) async-start(f32[3,8,32,512]{3,2,0,1:T(8,128)} %bitcast_add_fusion.1), calls=%async_computation.1 | async-start | bytes 3145728 | tf_op jit(solution)/shard_map/all_to_all | solution.py:121
  111.1 3.0 %copy-start.7 = (f32[3,1,32,512]{3,2,1,0:T(8,128)S(1)}, f32[3,1,32,512]{3,2,1,0:T(8,128)}, u32[]{:S(2)}) copy-start(f32[3,1,32,512]{3,2,1,0:T(8,128)} %param.8) | copy-start | bytes 589828
  111.1 3.1 %copy-start.9 = (f32[3,32,512]{2,1,0:T(8,128)S(1)}, f32[3,32,512]{2,1,0:T(8,128)}, u32[]{:S(2)}) copy-start(f32[3,32,512]{2,1,0:T(8,128)} %copy-done.8) | copy-start | bytes 589828
  112.5 14.1 %collective-permute-start.6 = (f32[3,2,32,512]{3,2,0,1:T(8,128)S(1)}, f32[3,2,32,512]{3,2,0,1:T(8,128)S(1)}, u32[]{:S(2)}, u32[]{:S(2)}) collective-permute-start(f32[3,2,32,512]{3,2,0,1:T(8,128)S(1)} %dynamic-slice_bitcast_fusion.1), channel_id=1, source_target_pairs={{0,32},{16,48},{32,0},{48,16},{64,96},{80,112},{96,64},{112,80},{1... | collective-permute-start | bytes 1179656 | tf_op jit(solution)/shard_map/ppermute | solution.py:133
  115.0 33.7 %collective-permute-start.9 = (f32[3,32,1024]{2,1,0:T(8,128)}, f32[3,32,1024]{2,1,0:T(8,128)}, u32[]{:S(2)}, u32[]{:S(2)}) collective-permute-start(f32[3,32,1024]{2,1,0:T(8,128)} %pad_maximum_fusion.2), channel_id=1, source_target_pairs={{0,0},{1,8},{2,16},{3,24},{4,32},{5,40},{6,48},{7,56},{8,1},{9,9},... | collective-permute-start | bytes 1179656 | tf_op jit(solution)/shard_map/ppermute | solution.py:81
  126.7 22.0 %collective-permute-start.7 = (f32[3,32,512]{2,1,0:T(8,128)S(1)}, f32[3,32,512]{2,1,0:T(8,128)S(1)}, u32[]{:S(2)}, u32[]{:S(2)}) collective-permute-start(f32[3,32,512]{2,1,0:T(8,128)S(1)} %dynamic-slice_bitcast_fusion.2), channel_id=1, source_target_pairs={{0,16},{16,0},{32,48},{48,32},{64,80},{80,64},{96,112},{112,96},{1... | collective-permute-start | bytes 589832 | tf_op jit(solution)/shard_map/ppermute | solution.py:133
  155.0 2.4 %collective-permute-start.10 = (f32[64,2560]{1,0:T(8,128)S(1)}, f32[64,2560]{1,0:T(8,128)S(1)}, u32[]{:S(2)}, u32[]{:S(2)}) collective-permute-start(f32[64,2560]{1,0:T(8,128)S(1)} %bitcast.216), channel_id=1, source_target_pairs={{0,8},{8,0},{1,9},{9,1},{2,10},{10,2},{3,11},{11,3},{4,12},{12,4},... | collective-permute-start | bytes 1966088 | tf_op jit(solution)/shard_map/ppermute | solution.py:57
  200.0 25.4 %collective-permute-start.11 = (f32[64,2560]{1,0:T(8,128)S(1)}, f32[64,2560]{1,0:T(8,128)S(1)}, u32[]{:S(2)}, u32[]{:S(2)}) collective-permute-start(f32[64,2560]{1,0:T(8,128)S(1)} %bitcast.215), channel_id=1, source_target_pairs={{0,8},{8,0},{1,9},{9,1},{2,10},{10,2},{3,11},{11,3},{4,12},{12,4},... | collective-permute-start | bytes 1966088 | tf_op jit(solution)/shard_map/ppermute | solution.py:187
  200.1 24.5 %collective-permute-start.8 = (f32[3,32,1024]{2,1,0:T(8,128)S(1)}, f32[3,32,1024]{2,1,0:T(8,128)S(1)}, u32[]{:S(2)}, u32[]{:S(2)}) collective-permute-start(f32[3,32,1024]{2,1,0:T(8,128)S(1)} %pad_maximum_fusion.1), channel_id=1, source_target_pairs={{0,0},{8,1},{16,2},{24,3},{32,4},{40,5},{48,6},{56,7},{1,8},{9,9},... | collective-permute-start | bytes 1179656 | tf_op jit(solution)/shard_map/ppermute | solution.py:178
  (2 other events, 2.8 us)

commit v2 on v0

--- a/solution.py
+++ b/solution.py
@@ -129,12 +129,14 @@
         )
 
     total = jnp.concatenate(
-        [
-            reduce_inner(x[..., k * PIECE:(k + 1) * PIECE], k > 0)
-            for k in range(2 * width // PIECE)
-        ],
+        [reduce_inner(x[..., k * PIECE:(k + 1) * PIECE], k > 0) for k in range(2 * width // PIECE)],
         axis=-1,
     )
+
+    def second_part(a, b):
+        return jnp.einsum(
+            "lsw,lsv->wv", a, b, precision=highest, preferred_element_type=jnp.float32
+        )
 
     owner_row = col_index + col_count * (row_index // col_count)
     kept_first = kept_of(pattern_first, owner_row)
@@ -155,12 +157,9 @@
                 precision=highest,
                 preferred_element_type=jnp.float32,
             ),
-            jnp.einsum(
-                "lsw,lsv->wv",
+            second_part(
                 x_at_reducer[..., width:],
                 column[..., width:],
-                precision=highest,
-                preferred_element_type=jnp.float32,
             ),
         ]
     )

time: 234 us -> 234 us (level)
  no operation moved by 1% of the time
where the time goes in v2:
time: 234 us; the launch traced here: 232 us
  waiting for transfers between devices  100 us (43%)
  blocking collectives  38.3 us (16%)
  starting transfers between devices  36.5 us (16%)
  matrix products  22 us (9%)
  other arithmetic  17.1 us (7%)
  local copies, waits for them, and re-layouts  16.7 us (7%)
    all_to_all x2, waiting for transfers between devices, reduce_gathered(): received = lax.all_to_all(pre, 'prow_hi', 1, 1, tiled=True)  30.3 us
    ppermute x3, waiting for transfers between devices, gather_piece(): lax.ppermute(held, 'pcol', [(i, i ^ 1 << b) for i in range(col_count)])  24.6 us
    all_to_all x1, blocking collectives, body(): reduced = jnp.sum(lax.all_to_all(flat, others, 0, 0, tiled=True), axis=0)  20.2 us
    ppermute x1, waiting for transfers between devices, body(): column_home = lax.ppermute(column, both, to_owner)  19.4 us
    all_to_all x1, blocking collectives, body(): lax.all_to_all(spread_sum, others, 0, 0, tiled=True).reshape(half.shape)  18.1 us
    dot_general x2, matrix products, product_of(): jnp.einsum('lsmt,lsw->mtw', matrix, gathered, precision=highest, preferre...  18.1 us
    ppermute x1, waiting for transfers between devices, body(): x_at_reducer = lax.ppermute(x, both, to_reducer)  17.5 us
    all_to_all x2, starting transfers between devices, reduce_gathered(): received = lax.all_to_all(pre, 'prow_hi', 1, 1, tiled=True)  13.6 us
  transfers between devices with their start and end apart: 12, of which 9 were waited for; matrix products, arithmetic and copies ran while one was open for 15% of the time, Pallas kernels for 0%

profile of v2, /device:TPU:6, one launch (start us, length us, event | category | flops | bytes accessed | tf_op | source)
XLA Modules:
  0.0 232.2 jit_solution(6822407111641995977)
XLA Ops:
  3.4 4.0 %collective-permute-start.1 = (f32[3,32,512]{2,1,0:T(8,128)S(1)}, f32[3,32,512]{2,1,0:T(8,128)S(1)}, u32[]{:S(2)}, u32[]{:S(2)}) collective-permute-start(f32[3,32,512]{2,1,0:T(8,128)S(1)} %bitcast_multiply_fusion.1), channel_id=1, source_target_pairs={{0,2},{1,3},{2,0},{3,1},{4,6},{5,7},{6,4},{7,5},{8,10},{9,11},{10,... | collective-permute-start | bytes 589832 | tf_op jit(solution)/shard_map/ppermute | solution.py:97
  8.4 3.9 %collective-permute-done.1 = f32[3,32,512]{2,1,0:T(8,128)S(1)} collective-permute-done((f32[3,32,512]{2,1,0:T(8,128)S(1)}, f32[3,32,512]{2,1,0:T(8,128)S(1)}, u32[]{:S(2)}, u32[]{:S(2)}) %collective-permute-start.1) | collective-permute-done | bytes 196640 | tf_op jit(solution)/shard_map/ppermute | solution.py:97
  13.8 8.9 %collective-permute-done.2 = f32[2,3,32,512]{3,2,1,0:T(8,128)S(1)} collective-permute-done((f32[2,3,32,512]{3,2,1,0:T(8,128)S(1)}, f32[2,3,32,512]{3,2,1,0:T(8,128)S(1)}, u32[]{:S(2)}, u32[]{:S(2)}) %collective-permute-start.2) | collective-permute-done | bytes 393248 | tf_op jit(solution)/shard_map/ppermute | solution.py:97
  26.5 6.0 %all-to-all-start = ((f32[3,256,512]{2,0,1:T(4,128)}), f32[3,256,512]{2,0,1:T(4,128)S(1)}, u32[]{:S(2)}, u32[]{:S(2)}) async-start(f32[3,256,512]{2,0,1:T(4,128)} %bitcast.1), calls=%async_computation | async-start | bytes 4194304 | tf_op jit(solution)/shard_map/all_to_all | solution.py:112
  32.6 11.8 %collective-permute-done.3 = f32[2,2,3,32,512]{4,3,2,0,1:T(8,128)} collective-permute-done((f32[2,2,3,32,512]{4,3,2,0,1:T(8,128)}, f32[2,2,3,32,512]{4,3,2,0,1:T(8,128)}, u32[]{:S(2)}, u32[]{:S(2)}) %collective-permute-start.3) | collective-permute-done | bytes 786464 | tf_op jit(solution)/shard_map/ppermute | solution.py:97
  47.1 7.7 %fusion = f32[512,6,256,1]{0,2,3,1:T(8,128)S(1)} fusion(f32[3,256,512,1]{2,1,0,3:T(8,128)S(1)} %bitcast.185, f32[3,1,256,6,1,256]{5,4,3,2,1,0:T(1,128)S(1)} %bitcast.181), kind=kOutput, calls=%fused_computation | convolution fusion | flops 7247757312 | bytes 9437184 | tf_op jit(solution)/shard_map/lsmt,lsw->mtw/dot_general | solution.py:123
  57.6 6.6 %all-to-all-done = f32[3,256,512]{2,0,1:T(4,128)S(1)} async-done(((f32[3,256,512]{2,0,1:T(4,128)}), f32[3,256,512]{2,0,1:T(4,128)S(1)}, u32[]{:S(2)}, u32[]{:S(2)}) %all-to-all-start) | async-done | bytes 1572896 | tf_op jit(solution)/shard_map/all_to_all | solution.py:112
  64.2 10.4 %fusion.2 = f32[512,6,256,1]{0,2,3,1:T(8,128)S(1)} fusion(f32[3,1,256,6,1,256]{5,4,3,2,1,0:T(1,128)} %param.7, f32[3,256,512]{2,0,1:T(4,128)S(1)} %all-to-all-done), kind=kOutput, calls=%fused_computation.2 | convolution fusion | flops 7247757312 | bytes 9437184 | tf_op jit(solution)/shard_map/lsmt,lsw->mtw/dot_general | solution.py:123
  76.9 2.9 %bitcast_add_fusion = f32[3,8,32,512]{3,2,0,1:T(8,128)} fusion(f32[3,8,32,512]{3,2,0,1:T(8,128)} %collective-permute-done.4, f32[3,8,1,32,512]{4,3,2,1,0:T(8,128)S(1)} %copy-done), kind=kLoop, calls=%fused_computation.8 | loop fusion | flops 393216 | bytes 4718592 | tf_op jit(solution)/shard_map/add | solution.py:57
  79.8 7.4 %all-to-all-start.2 = ((f32[3,8,32,512]{3,2,0,1:T(8,128)}), f32[3,8,32,512]{3,2,0,1:T(8,128)S(1)}, u32[]{:S(2)}, u32[]{:S(2)}) async-start(f32[3,8,32,512]{3,2,0,1:T(8,128)} %bitcast_add_fusion), calls=%async_computation.2 | async-start | bytes 3145728 | tf_op jit(solution)/shard_map/all_to_all | solution.py:119
  87.3 2.9 %bitcast_add_fusion.1 = f32[3,8,32,512]{3,2,0,1:T(8,128)} fusion(f32[3,8,32,512]{3,2,0,1:T(8,128)} %collective-permute-done, f32[3,8,1,32,512]{4,3,2,1,0:T(8,128)S(1)} %get-tuple-element.8), kind=kLoop, calls=%fused_computation.9 | loop fusion | flops 393216 | bytes 4718592 | tf_op jit(solution)/shard_map/add | solution.py:57
  90.2 17.3 %all-to-all-done.2 = f32[3,8,32,512]{3,2,0,1:T(8,128)S(1)} async-done(((f32[3,8,32,512]{3,2,0,1:T(8,128)}), f32[3,8,32,512]{3,2,0,1:T(8,128)S(1)}, u32[]{:S(2)}, u32[]{:S(2)}) %all-to-all-start.2) | async-done | bytes 1572896 | tf_op jit(solution)/shard_map/all_to_all | solution.py:119
  107.4 6.2 %all-to-all-start.1 = ((f32[3,8,32,512]{3,2,0,1:T(8,128)}), f32[3,8,32,512]{3,2,0,1:T(8,128)S(1)}, u32[]{:S(2)}, u32[]{:S(2)}) async-start(f32[3,8,32,512]{3,2,0,1:T(8,128)} %bitcast_add_fusion.1), calls=%async_computation.1 | async-start | bytes 3145728 | tf_op jit(solution)/shard_map/all_to_all | solution.py:119
  114.5 5.5 %collective-permute-start.6 = (f32[3,32,1024]{2,1,0:T(8,128)}, f32[3,32,1024]{2,1,0:T(8,128)}, u32[]{:S(2)}, u32[]{:S(2)}) collective-permute-start(f32[3,32,1024]{2,1,0:T(8,128)} %pad_maximum_fusion.2), channel_id=1, source_target_pairs={{0,0},{1,8},{2,16},{3,24},{4,32},{5,40},{6,48},{7,56},{8,1},{9,9},... | collective-permute-start | bytes 1179656 | tf_op jit(solution)/shard_map/ppermute | solution.py:81
  120.1 13.1 %all-to-all-done.1 = f32[3,8,32,512]{3,2,0,1:T(8,128)S(1)} async-done(((f32[3,8,32,512]{3,2,0,1:T(8,128)}), f32[3,8,32,512]{3,2,0,1:T(8,128)S(1)}, u32[]{:S(2)}, u32[]{:S(2)}) %all-to-all-start.1) | async-done | bytes 1572896 | tf_op jit(solution)/shard_map/all_to_all | solution.py:119
  133.5 17.5 %collective-permute-done.6 = f32[3,32,1024]{2,1,0:T(8,128)} collective-permute-done((f32[3,32,1024]{2,1,0:T(8,128)}, f32[3,32,1024]{2,1,0:T(8,128)}, u32[]{:S(2)}, u32[]{:S(2)}) %collective-permute-start.6) | collective-permute-done | bytes 393248 | tf_op jit(solution)/shard_map/ppermute | solution.py:81
  151.0 2.0 convolution_bitcast_fusion
  152.9 2.0 convolution_bitcast_fusion.1
  157.3 2.1 collective-permute-done.7
  159.9 20.2 %all_to_all.33 = f32[64,1,2560]{2,1,0:T(1,128)S(1)} all-to-all(f32[64,1,2560]{2,1,0:T(1,128)S(1)} %all_to_all.24), channel_id=1, replica_groups=mesh['prow_hi'=8,'core'=2,'pcol'=8] {'prow_hi','pcol'}, dimensions={0} | all-to-all | bytes 1310720 | tf_op jit(solution)/shard_map/all_to_all | solution.py:172
  180.8 18.1 %all_to_all.34 = f32[64,1,2560]{2,1,0:T(1,128)S(1)} all-to-all(f32[64,1,2560]{2,1,0:T(1,128)S(1)} %broadcast_in_dim.28), channel_id=1, replica_groups=mesh['prow_hi'=8,'core'=2,'pcol'=8] {'prow_hi','pcol'}, dimensions={0} | all-to-all | bytes 1310720 | tf_op jit(solution)/shard_map/all_to_all | solution.py:174
  199.1 5.1 %collective-permute-start.5 = (f32[3,32,1024]{2,1,0:T(8,128)S(1)}, f32[3,32,1024]{2,1,0:T(8,128)S(1)}, u32[]{:S(2)}, u32[]{:S(2)}) collective-permute-start(f32[3,32,1024]{2,1,0:T(8,128)S(1)} %pad_maximum_fusion.1), channel_id=1, source_target_pairs={{0,0},{8,1},{16,2},{24,3},{32,4},{40,5},{48,6},{56,7},{1,8},{9,9},... | collective-permute-start | bytes 1179656 | tf_op jit(solution)/shard_map/ppermute | solution.py:166
  204.2 19.4 %collective-permute-done.5 = f32[3,32,1024]{2,1,0:T(8,128)S(1)} collective-permute-done((f32[3,32,1024]{2,1,0:T(8,128)S(1)}, f32[3,32,1024]{2,1,0:T(8,128)S(1)}, u32[]{:S(2)}, u32[]{:S(2)}) %collective-permute-start.5) | collective-permute-done | bytes 393248 | tf_op jit(solution)/shard_map/ppermute | solution.py:166
  224.9 1.9 maximum_select_fusion.1
  (91 shorter events, 28.4 us)
Async XLA Ops:
  0.6 13.1 %copy-start.1 = (f32[3,1,32,512]{3,2,1,0:T(8,128)S(1)}, f32[3,1,32,512]{3,2,1,0:T(8,128)}, u32[]{:S(2)}) copy-start(f32[3,1,32,512]{3,2,1,0:T(8,128)} %param.9) | copy-start | bytes 589828
  3.4 8.9 %copy-start.6 = (f32[3,32,512]{2,1,0:T(8,128)}, f32[3,32,512]{2,1,0:T(8,128)S(1)}, u32[]{:S(2)}) copy-start(f32[3,32,512]{2,1,0:T(8,128)S(1)} %bitcast_multiply_fusion.1) | copy-start | bytes 589828
  3.4 8.9 %collective-permute-start.1 = (f32[3,32,512]{2,1,0:T(8,128)S(1)}, f32[3,32,512]{2,1,0:T(8,128)S(1)}, u32[]{:S(2)}, u32[]{:S(2)}) collective-permute-start(f32[3,32,512]{2,1,0:T(8,128)S(1)} %bitcast_multiply_fusion.1), channel_id=1, source_target_pairs={{0,2},{1,3},{2,0},{3,1},{4,6},{5,7},{6,4},{7,5},{8,10},{9,11},{10,... | collective-permute-start | bytes 589832 | tf_op jit(solution)/shard_map/ppermute | solution.py:97
  12.3 12.2 %copy-start.4 = (f32[3,1,32,512]{3,2,1,0:T(8,128)S(1)}, f32[3,1,32,512]{3,2,1,0:T(8,128)}, u32[]{:S(2)}) copy-start(f32[3,1,32,512]{3,2,1,0:T(8,128)} %param.8) | copy-start | bytes 589828
  12.4 10.4 %collective-permute-start.2 = (f32[2,3,32,512]{3,2,1,0:T(8,128)S(1)}, f32[2,3,32,512]{3,2,1,0:T(8,128)S(1)}, u32[]{:S(2)}, u32[]{:S(2)}) collective-permute-start(f32[2,3,32,512]{3,2,1,0:T(8,128)S(1)} %maximum_select_fusion.5), channel_id=1, source_target_pairs={{0,1},{1,0},{2,3},{3,2},{4,5},{5,4},{6,7},{7,6},{8,9},{9,8},{10,11... | collective-permute-start | bytes 1179656 | tf_op jit(solution)/shard_map/ppermute | solution.py:97
  23.7 20.7 %collective-permute-start.3 = (f32[2,2,3,32,512]{4,3,2,0,1:T(8,128)}, f32[2,2,3,32,512]{4,3,2,0,1:T(8,128)}, u32[]{:S(2)}, u32[]{:S(2)}) collective-permute-start(f32[2,2,3,32,512]{4,3,2,0,1:T(8,128)} %maximum_select_fusion.3), channel_id=1, source_target_pairs={{0,4},{1,5},{2,6},{3,7},{4,0},{5,1},{6,2},{7,3},{8,12},{9,13},{10,... | collective-permute-start | bytes 2359304 | tf_op jit(solution)/shard_map/ppermute | solution.py:97
  26.5 20.0 %slice-start = ((s8[4718592]{0:T(1024)(128)(4,1)}), s8[524288]{0:T(1024)(128)(4,1)S(1)}, s32[]{:S(2)}) async-start(s8[4718592]{0:T(1024)(128)(4,1)} %bitcast.180), calls=%async_computation.5 | async-start | bytes 1048576
  26.5 37.7 %all-to-all-start = ((f32[3,256,512]{2,0,1:T(4,128)}), f32[3,256,512]{2,0,1:T(4,128)S(1)}, u32[]{:S(2)}, u32[]{:S(2)}) async-start(f32[3,256,512]{2,0,1:T(4,128)} %bitcast.1), calls=%async_computation | async-start | bytes 4194304 | tf_op jit(solution)/shard_map/all_to_all | solution.py:112
  44.4 2.7 %slice-start.1 = ((s8[4718592]{0:T(1024)(128)(4,1)}), s8[4194304]{0:T(1024)(128)(4,1)S(1)}, s32[]{:S(2)}) async-start(s8[4718592]{0:T(1024)(128)(4,1)} %bitcast.180), calls=%async_computation.6 | async-start | bytes 8388608
  57.6 18.7 %collective-permute-start.4 = (f32[3,8,32,512]{3,2,0,1:T(8,128)}, f32[3,8,32,512]{3,2,0,1:T(8,128)}, u32[]{:S(2)}, u32[]{:S(2)}) collective-permute-start(f32[3,8,32,512]{3,2,0,1:T(8,128)} %bitcast.176), channel_id=1, source_target_pairs={{0,8},{8,0},{1,9},{9,1},{2,10},{10,2},{3,11},{11,3},{4,12},{12,4},... | collective-permute-start | bytes 4718600 | tf_op jit(solution)/shard_map/ppermute | solution.py:57
  74.9 2.0 copy-start
  76.2 11.0 %collective-permute-start = (f32[3,8,32,512]{3,2,0,1:T(8,128)}, f32[3,8,32,512]{3,2,0,1:T(8,128)}, u32[]{:S(2)}, u32[]{:S(2)}) collective-permute-start(f32[3,8,32,512]{3,2,0,1:T(8,128)} %bitcast.177), channel_id=1, source_target_pairs={{0,8},{8,0},{1,9},{9,1},{2,10},{10,2},{3,11},{11,3},{4,12},{12,4},... | collective-permute-start | bytes 4718600 | tf_op jit(solution)/shard_map/ppermute | solution.py:57
  79.8 27.6 %all-to-all-start.2 = ((f32[3,8,32,512]{3,2,0,1:T(8,128)}), f32[3,8,32,512]{3,2,0,1:T(8,128)S(1)}, u32[]{:S(2)}, u32[]{:S(2)}) async-start(f32[3,8,32,512]{3,2,0,1:T(8,128)} %bitcast_add_fusion), calls=%async_computation.2 | async-start | bytes 3145728 | tf_op jit(solution)/shard_map/all_to_all | solution.py:119
  90.2 23.5 %copy-start.5 = (f32[3,1,32,512]{3,2,1,0:T(8,128)S(1)}, f32[3,1,32,512]{3,2,1,0:T(8,128)}, u32[]{:S(2)}) copy-start(f32[3,1,32,512]{3,2,1,0:T(8,128)} %param.8) | copy-start | bytes 589828
  90.2 23.6 %copy-start.7 = (f32[3,32,512]{2,1,0:T(8,128)S(1)}, f32[3,32,512]{2,1,0:T(8,128)}, u32[]{:S(2)}) copy-start(f32[3,32,512]{2,1,0:T(8,128)} %copy-done.6) | copy-start | bytes 589828
  107.4 25.7 %all-to-all-start.1 = ((f32[3,8,32,512]{3,2,0,1:T(8,128)}), f32[3,8,32,512]{3,2,0,1:T(8,128)S(1)}, u32[]{:S(2)}, u32[]{:S(2)}) async-start(f32[3,8,32,512]{3,2,0,1:T(8,128)} %bitcast_add_fusion.1), calls=%async_computation.1 | async-start | bytes 3145728 | tf_op jit(solution)/shard_map/all_to_all | solution.py:119
  114.5 36.5 %collective-permute-start.6 = (f32[3,32,1024]{2,1,0:T(8,128)}, f32[3,32,1024]{2,1,0:T(8,128)}, u32[]{:S(2)}, u32[]{:S(2)}) collective-permute-start(f32[3,32,1024]{2,1,0:T(8,128)} %pad_maximum_fusion.2), channel_id=1, source_target_pairs={{0,0},{1,8},{2,16},{3,24},{4,32},{5,40},{6,48},{7,56},{8,1},{9,9},... | collective-permute-start | bytes 1179656 | tf_op jit(solution)/shard_map/ppermute | solution.py:81
  157.2 2.2 collective-permute-start.7
  199.0 25.4 %collective-permute-start.8 = (f32[64,2560]{1,0:T(8,128)S(1)}, f32[64,2560]{1,0:T(8,128)S(1)}, u32[]{:S(2)}, u32[]{:S(2)}) collective-permute-start(f32[64,2560]{1,0:T(8,128)S(1)} %bitcast.195), channel_id=1, source_target_pairs={{0,8},{8,0},{1,9},{9,1},{2,10},{10,2},{3,11},{11,3},{4,12},{12,4},... | collective-permute-start | bytes 1966088 | tf_op jit(solution)/shard_map/ppermute | solution.py:175
  199.1 24.5 %collective-permute-start.5 = (f32[3,32,1024]{2,1,0:T(8,128)S(1)}, f32[3,32,1024]{2,1,0:T(8,128)S(1)}, u32[]{:S(2)}, u32[]{:S(2)}) collective-permute-start(f32[3,32,1024]{2,1,0:T(8,128)S(1)} %pad_maximum_fusion.1), channel_id=1, source_target_pairs={{0,0},{8,1},{16,2},{24,3},{32,4},{40,5},{48,6},{56,7},{1,8},{9,9},... | collective-permute-start | bytes 1179656 | tf_op jit(solution)/shard_map/ppermute | solution.py:166
  228.9 1.2 copy-start.2
  228.9 1.5 copy-start.3
